TPU v7x, 32 devices: a whole 2x2x4 slice. The times are simulated.
32 devices in a mesh: rep: 4 (over z), tp: 8 (over y, x, core).
Axes of the slice: x: 2, y: 2, z: 4, core: 2. Of those that a mesh axis runs over, the one named last changes fastest.
Arguments:
- activations: bfloat16 [6144, 1024], P(('rep', 'tp')), may hold values from -6 to 6
- out_grads: bfloat16 [6144, 3072], P('rep', 'tp'), may hold values from -0.15625 to 0.15625
- error_state: bfloat16 [4, 1024, 3072], P('rep', None, 'tp'), may hold values from -4 to 4
- q_start: float32 [3072, 32], P('tp'), may hold values from -6 to 6
- qkv_master: float32 [1024, 3072], P('rep', 'tp'), may hold values from -3 to 3
- qkv_moment: float32 [1024, 3072], P('rep', 'tp'), may hold values from -0.75 to 0.75
- word_grads: bfloat16 [6144, 1024], P('rep', 'tp'), may hold values from -6 to 6
- token_ids: int32 [6144], P('rep'), may hold values from 0 to 1599, as said below
- owner_map: int32 [1600], replicated, may hold values from 0 to 1599, as said below
- word_master: float32 [1600, 1024], P('rep', 'tp'), may hold values from -6 to 6
Outputs:
- error_new: bfloat16 [4, 1024, 3072], P('rep', None, 'tp')
- q_factor: float32 [3072, 32], P('tp')
- moment_new: float32 [1024, 3072], P('rep', 'tp')
- master_new: float32 [1024, 3072], P('rep', 'tp')
- weight_bf16: bfloat16 [1024, 3072], P(None, 'tp')
- word_new: float32 [1600, 1024], P('rep', 'tp')
Inputs may be any that keep to these rules, and one draw needn't show every extreme that they name: A permutation of the rows: word w is stored in row owner_map[w] of word_master, whose owner is that row divided by 400. `token_ids`: the 1536 tokens of one replica name words of one owner at most 768 times; in every replica some owner is named exactly 768 times.
All inputs are finite; a program needn't handle non-finite values.
Results may differ from a plain program's by a relative error of at most 0.001.
Values may be sent and summed in bfloat16 or wider, within the bound.
No kernel may reach another device: no remote copies, remote signals or barrier semaphores. Data moves between devices by JAX's collectives and lax.ppermute only.
A program may use at most 64 MiB of HBM per device.

v0:
```python
import jax
import jax.numpy as jnp
from jax import lax
from jax.sharding import PartitionSpec as P

ROUNDS = 2
MOMENTUM = 0.9
LEARNING_RATE = 4.0
EMBED_RATE = 0.5


def orthonormal(left_basis, gram_matrix):
    factor_low = jnp.linalg.cholesky(gram_matrix)
    return jax.scipy.linalg.solve_triangular(factor_low, left_basis.T, lower=True).T


def word_update(word_grads, token_ids, owner_map, word_master):
    replicas = lax.axis_size("rep")
    per_owner = word_master.shape[0]
    capacity = 2 * token_ids.shape[0] // replicas
    targets = owner_map[token_ids]
    owners = targets // per_owner
    row_slot = targets % per_owner
    matches = (owners[:, None] == jnp.arange(replicas, dtype=jnp.int32)[None, :]).astype(jnp.int32)
    places = jnp.sum(jnp.cumsum(matches, axis=0) * matches, axis=1) - 1
    outgoing = (
        jnp.zeros((replicas, capacity, word_grads.shape[1]), jnp.bfloat16)
        .at[owners, places]
        .set(word_grads)
    )
    labels = jnp.full((replicas, capacity), per_owner, jnp.int32).at[owners, places].set(row_slot)
    incoming, arrived = (
        lax.all_to_all(outgoing, "rep", split_axis=0, concat_axis=0, tiled=True),
        lax.all_to_all(labels, "rep", split_axis=0, concat_axis=0, tiled=True),
    )
    flat_rows = incoming.reshape(-1, incoming.shape[2])
    selector = (
        arrived.reshape(-1)[:, None] == jnp.arange(per_owner, dtype=jnp.int32)[None, :]
    ).astype(jnp.bfloat16)
    row_grad = lax.dot_general(
        selector, flat_rows, (((0,), (0,)), ((), ())), preferred_element_type=jnp.float32
    )
    return word_master - EMBED_RATE * row_grad


def shards(
    activations,
    out_grads,
    error_state,
    q_start,
    qkv_master,
    qkv_moment,
    word_grads,
    token_ids,
    owner_map,
    word_master,
):
    highest = lax.Precision.HIGHEST
    replicas = lax.axis_size("rep")
    word_new = None
    product = lax.dot_general(
        lax.all_gather(activations, "tp", axis=0, tiled=True),
        out_grads,
        (((0,), (0,)), ((), ())),
        preferred_element_type=jnp.float32,
    )
    combined = product + error_state[0].astype(jnp.float32)
    right_basis = q_start
    left_basis = None
    for round_index in range(ROUNDS):
        partial_left = jnp.dot(combined, right_basis, precision=highest)
        left_basis = lax.psum(partial_left, ("rep", "tp")) / replicas
        gram_matrix = jnp.dot(left_basis.T, left_basis, precision=highest)
        left_basis = orthonormal(left_basis, gram_matrix)
        partial_right = lax.dot_general(
            combined, left_basis, (((0,), (0,)), ((), ())), precision=highest
        )
        right_basis = lax.psum(partial_right, "rep") / replicas
    approx = jnp.dot(left_basis, right_basis.T, precision=highest)
    error_new = (combined - approx).astype(jnp.bfloat16)[None]
    owned_rows = qkv_master.shape[0]
    update_rows = lax.dynamic_slice_in_dim(
        approx, lax.axis_index("rep") * owned_rows, owned_rows, 0
    )
    moment_new = MOMENTUM * qkv_moment + update_rows
    master_new = qkv_master - LEARNING_RATE * moment_new
    weight_bf16 = lax.all_gather(master_new.astype(jnp.bfloat16), "rep", axis=0, tiled=True)
    word_new = word_update(word_grads, token_ids, owner_map, word_master)
    return (error_new, right_basis, moment_new, master_new, weight_bf16, word_new)


def solution(mesh):
    in_specs = (
        P(("rep", "tp"), None),
        P("rep", "tp"),
        P("rep", None, "tp"),
        P("tp", None),
        P("rep", "tp"),
        P("rep", "tp"),
        P("rep", "tp"),
        P("rep"),
        P(),
        P("rep", "tp"),
    )
    out_specs = (
        P("rep", None, "tp"),
        P("tp", None),
        P("rep", "tp"),
        P("rep", "tp"),
        P(None, "tp"),
        P("rep", "tp"),
    )
    return jax.shard_map(shards, mesh=mesh, in_specs=in_specs, out_specs=out_specs, check_vma=False)
```

profile of v0, /device:TPU:0, one launch (start us, length us, event | category | flops | bytes accessed | tf_op | source)
XLA Modules:
  0.0 393.2 jit_solution(7987979019762832987)
XLA Ops:
  8.0 0.7 compare_select_fusion.2
  8.7 8.4 %gather_fusion = s32[1536]{0:T(1024)S(1)} fusion(s32[1600]{0:T(1024)S(1)} %copy-done.1, s32[2048]{0:T(1024)S(1)} %pad_clamp_fusion), kind=kCustom, calls=%fused_computation | custom fusion | bytes 18432 | tf_op jit(solution)/shard_map/gather | solution.py:21
  17.2 1.2 reduce-window.6
  19.1 25.9 %all-gather.2.cloned.1.call-done = bf16[1536,1024]{1,0:T(8,128)(2,1)} async-done(((bf16[192,1024]{1,0:T(8,128)(2,1)}), bf16[1536,1024]{1,0:T(8,128)(2,1)}) %all-gather.2.cloned.1.call-update) | async-done | bytes 3145744 | tf_op jit(solution)/shard_map/all_gather | solution.py:62
  45.0 3.9 convert_add_fusion
  48.9 2.2 fusion.45
  51.2 6.8 %scatter_custom_fusion = s32[3072]{0:T(1024)} fusion(s32[1536]{0:T(1024)S(1)} %broadcast_select_fusion, s32[1536]{0:T(1024)S(1)} %get-tuple-element.13, s32[]{:T(128)} %constant.83.clone.1), kind=kCustom, calls=%fused_computation.70 | custom fusion | bytes 12292
  57.9 4.6 %all-to-all-start = ((s32[4,1,768]{2,1,0:T(1,128)}), s32[4,1,768]{2,1,0:T(1,128)S(1)}, u32[]{:S(2)}, u32[]{:S(2)}) async-start(s32[4,1,768]{2,1,0:T(1,128)} %bitcast.13), calls=%async_computation | async-start | bytes 24576 | tf_op jit(solution)/shard_map/all_to_all | solution.py:34
  62.5 5.7 %scatter_custom_fusion.1 = bf16[3072,128]{1,0:T(8,128)(2,1)} fusion(s32[1536]{0:T(1024)S(1)} %broadcast_select_fusion, bf16[1536,128]{1,0:T(8,128)(2,1)} %param.19, bf16[]{:T(256)} %constant.89.clone.1), kind=kCustom, calls=%fused_computation.11 | custom fusion | bytes 786944
  68.3 105.5 %all-reduce.3.cloned.1.call-done = f32[1024,32]{0,1:T(8,128)} async-done(((f32[1024,32]{0,1:T(8,128)}), f32[1024,32]{0,1:T(8,128)}) %all-reduce.3.cloned.1.call-update) | async-done | bytes 131088 | tf_op jit(solution)/shard_map/psum | solution.py:72
  173.8 1.2 fusion.15
  175.1 2.9 cholesky.44
  178.6 3.6 all-to-all-start.1
  182.9 1.3 fusion.27
  184.1 3.2 custom-call.6
  187.3 1.2 fusion.9
  188.5 1.6 fusion.46
  190.1 21.4 %psum.29 = f32[384,32]{0,1:T(8,128)} all-reduce(f32[384,32]{0,1:T(8,128)} %fusion.46), channel_id=1, replica_groups=mesh['rep'=4,'tp'=8] {'rep'}, use_global_device_ids=true, to_apply=%region_3.0 | all-reduce | flops 12288 | bytes 98304 | tf_op jit(solution)/shard_map/psum | solution.py:78
  211.5 3.0 fusion.21
  214.6 2.5 fusion.3
  217.1 119.1 %all-reduce.5.cloned.1.call-done = f32[1024,32]{0,1:T(8,128)} async-done(((f32[1024,32]{0,1:T(8,128)}), f32[1024,32]{0,1:T(8,128)}) %all-reduce.5.cloned.1.call-update) | async-done | bytes 131088 | tf_op jit(solution)/shard_map/psum | solution.py:72
  336.1 1.2 fusion.12
  337.4 2.9 cholesky.55
  341.7 2.4 custom-call.7
  344.1 1.2 fusion.7
  345.4 1.0 fusion.47
  346.4 18.4 %psum.31 = f32[384,32]{0,1:T(8,128)S(1)} all-reduce(f32[384,32]{0,1:T(8,128)S(1)} %fusion.47), channel_id=1, replica_groups=mesh['rep'=4,'tp'=8] {'rep'}, use_global_device_ids=true, to_apply=%region_5.8 | all-reduce | flops 12288 | bytes 98304 | tf_op jit(solution)/shard_map/psum | solution.py:78
  364.8 1.5 fusion.48
  366.3 1.1 fusion.4
  367.4 1.0 fusion.44
  368.4 17.4 %all_gather.7 = bf16[1024,384]{1,0:T(8,128)(2,1)S(1)} all-gather(bf16[256,384]{1,0:T(8,128)(2,1)S(1)} %get-tuple-element.10), channel_id=1, replica_groups=mesh['rep'=4,'tp'=8] {'rep'}, dimensions={0}, use_global_device_ids=true | all-gather | bytes 983040 | tf_op jit(solution)/shard_map/all_gather | solution.py:87
  385.8 0.9 copy.27
  (51 shorter events, 4.4 us)
Async XLA Ops:
  7.2 37.8 %copy-start = (bf16[1536,384]{1,0:T(8,128)(2,1)S(1)}, bf16[1536,384]{1,0:T(8,128)(2,1)}, u32[]{:S(2)}) copy-start(bf16[1536,384]{1,0:T(8,128)(2,1)} %param.14) | copy-start | bytes 3538948
  7.2 1.5 copy-start.1
  7.2 37.8 %all-gather.2.cloned.1.call-start = ((), (), s32[]{:S(2)}) async-start(), calls=%async_computation.2 | async-start | bytes 3538944 | tf_op jit(solution)/shard_map/all_gather | solution.py:62
  7.9 165.8 %all-reduce.3.cloned.1.call-start = ((), (), s32[]{:S(2)}) async-start(), calls=%async_computation.3 | async-start | bytes 262144 | tf_op jit(solution)/shard_map/psum | solution.py:72
  8.7 10.2 %copy-start.9 = (s32[2]{0:T(128)S(1)}, s32[2]{0:T(128)}, u32[]{:S(2)}) copy-start(s32[2]{0:T(128)} %constant.92) | copy-start | bytes 28
  8.7 10.3 %copy-start.8 = (s32[2]{0:T(128)S(1)}, s32[2]{0:T(128)}, u32[]{:S(2)}) copy-start(s32[2]{0:T(128)} %constant.95) | copy-start | bytes 28
  19.1 29.8 %copy-start.5 = (f32[384,32]{0,1:T(8,128)S(1)}, f32[384,32]{0,1:T(8,128)}, u32[]{:S(2)}) copy-start(f32[384,32]{0,1:T(8,128)} %param.16) | copy-start | bytes 147460
  57.9 120.1 %all-to-all-start = ((s32[4,1,768]{2,1,0:T(1,128)}), s32[4,1,768]{2,1,0:T(1,128)S(1)}, u32[]{:S(2)}, u32[]{:S(2)}) async-start(s32[4,1,768]{2,1,0:T(1,128)} %bitcast.13), calls=%async_computation | async-start | bytes 24576 | tf_op jit(solution)/shard_map/all_to_all | solution.py:34
  178.0 0.6 copy-start.6
  178.6 35.9 %all-to-all-start.1 = ((bf16[4,768,128]{2,1,0:T(8,128)(2,1)}), bf16[4,768,128]{2,1,0:T(8,128)(2,1)S(1)}, u32[]{:S(2)}, u32[]{:S(2)}) async-start(bf16[4,768,128]{2,1,0:T(8,128)(2,1)} %bitcast.15), calls=%async_computation.1 | async-start | bytes 1572864 | tf_op jit(solution)/shard_map/all_to_all | solution.py:33
  182.2 153.9 %all-reduce.5.cloned.1.call-start = ((), (), s32[]{:S(2)}) async-start(), calls=%async_computation.4 | async-start | bytes 262144 | tf_op jit(solution)/shard_map/psum | solution.py:72
  188.5 26.1 %copy-start.7 = (s32[4,1,768]{2,1,0:T(1,128)S(1)}, s32[4,1,768]{2,1,0:T(1,128)}, u32[]{:S(2)}) copy-start(s32[4,1,768]{2,1,0:T(1,128)} %copy-done.6) | copy-start | bytes 36868
  364.8 2.6 copy-start.4
  366.3 1.2 copy-start.2
  366.3 1.2 copy-start.3
Sparse Core Ops, SparseCore 0:
  9.9 35.0 all-gather.1
  51.3 122.4 all-reduce.2
  214.7 121.4 all-reduce.4
where the time goes:
time: 394 us; the launch traced here: 393 us
  waiting for transfers between devices  251 us (64%)
  blocking collectives  57.2 us (15%)
  local copies, waits for them, and re-layouts  22.8 us (6%)
  matrix products  20.6 us (5%)
  other arithmetic  19.2 us (5%)
  between operations  14 us (4%)
  starting transfers between devices  8.25 us (2%)
    psum x2, waiting for transfers between devices, shards(): left_basis = lax.psum(partial_left, ('rep', 'tp')) / replicas  225 us
    psum x2, blocking collectives, shards(): right_basis = lax.psum(partial_right, 'rep') / replicas  39.8 us
    all_gather x1, waiting for transfers between devices, shards(): lax.all_gather(activations, 'tp', axis=0, tiled=True)  25.9 us
    all_gather x1, blocking collectives, shards(): lax.all_gather(master_new.astype(jnp.bfloat16), 'rep', axis=0, tiled=True)  17.4 us
    unnamed x23, local copies, waits for them, and re-layouts  14 us
    gather x1, local copies, waits for them, and re-layouts, word_update(): targets = owner_map[token_ids]  8.39 us
  transfers between devices with their start and end apart: 5, of which 3 were waited for; matrix products, arithmetic and copies ran while one was open for 10% of the time, Pallas kernels for 0%

commit v1 on v0

--- a/solution.py
+++ b/solution.py
@@ -7,6 +7,11 @@
 MOMENTUM = 0.9
 LEARNING_RATE = 4.0
 EMBED_RATE = 0.5
+
+
+def one_after_other(array, first, second):
+    inner = lax.psum(array, first)
+    return lax.psum(inner, second)
 
 
 def orthonormal(left_basis, gram_matrix):
@@ -69,7 +74,7 @@
     left_basis = None
     for round_index in range(ROUNDS):
         partial_left = jnp.dot(combined, right_basis, precision=highest)
-        left_basis = lax.psum(partial_left, ("rep", "tp")) / replicas
+        left_basis = one_after_other(partial_left, "tp", "rep") / replicas
         gram_matrix = jnp.dot(left_basis.T, left_basis, precision=highest)
         left_basis = orthonormal(left_basis, gram_matrix)
         partial_right = lax.dot_general(

time: 394 us -> 327 us (0.83)
  waiting for transfers between devices: 251 us -> 183 us
    psum x2 -> x4, waiting for transfers between devices: 225 us -> 157 us  [the longest x2 104 us: one_after_other(): inner = lax.psum(array, first)]
  transfers between devices with their start and end apart: 5 -> 7, of which waited for: 3 -> 5; matrix products, arithmetic and copies ran while one was open for 10% -> 13% of each run, Pallas kernels for 0% -> 0%
where the time goes in v1:
time: 327 us; the launch traced here: 326 us
  waiting for transfers between devices  183 us (56%)
  blocking collectives  56.7 us (17%)
  local copies, waits for them, and re-layouts  22.8 us (7%)
  matrix products  20.6 us (6%)
  other arithmetic  20.4 us (6%)
  between operations  14.1 us (4%)
  starting transfers between devices  8.48 us (3%)
    psum x2, waiting for transfers between devices, one_after_other(): inner = lax.psum(array, first)  104 us
    psum x2, waiting for transfers between devices, one_after_other(): return lax.psum(inner, second)  52.8 us
    psum x2, blocking collectives, shards(): right_basis = lax.psum(partial_right, 'rep') / replicas  39.2 us
    all_gather x1, waiting for transfers between devices, shards(): lax.all_gather(activations, 'tp', axis=0, tiled=True)  26 us
    all_gather x1, blocking collectives, shards(): lax.all_gather(master_new.astype(jnp.bfloat16), 'rep', axis=0, tiled=True)  17.5 us
    unnamed x23, local copies, waits for them, and re-layouts  14 us
    gather x1, local copies, waits for them, and re-layouts, word_update(): targets = owner_map[token_ids]  8.39 us
    another operation x6, other arithmetic, orthonormal(): factor_low = jnp.linalg.cholesky(gram_matrix)  8.37 us
  transfers between devices with their start and end apart: 7, of which 5 were waited for; matrix products, arithmetic and copies ran while one was open for 13% of the time, Pallas kernels for 0%

profile of v1, /device:TPU:0, one launch (start us, length us, event | category | flops | bytes accessed | tf_op | source)
XLA Modules:
  0.0 326.5 jit_solution(17459196841000662712)
XLA Ops:
  8.7 8.4 %gather_fusion = s32[1536]{0:T(1024)S(1)} fusion(s32[1600]{0:T(1024)S(1)} %copy-done.1, s32[2048]{0:T(1024)S(1)} %pad_clamp_fusion), kind=kCustom, calls=%fused_computation | custom fusion | bytes 18432 | tf_op jit(solution)/shard_map/gather | solution.py:26
  17.2 1.2 reduce-window.6
  19.0 26.0 %all-gather.2.cloned.1.call-done = bf16[1536,1024]{1,0:T(8,128)(2,1)} async-done(((bf16[192,1024]{1,0:T(8,128)(2,1)}), bf16[1536,1024]{1,0:T(8,128)(2,1)}) %all-gather.2.cloned.1.call-update) | async-done | bytes 3145744 | tf_op jit(solution)/shard_map/all_gather | solution.py:67
  45.0 3.9 %convert_add_fusion = f32[1024,384]{1,0:T(8,128)S(1)} fusion(bf16[1536,1024]{1,0:T(8,128)(2,1)} %all-gather.2.cloned.1.call-done, bf16[1536,384]{1,0:T(8,128)(2,1)S(1)} %copy-done, bf16[1,1024,384]{2,1,0:T(8,128)(2,1)} %param.15), kind=kOutput, calls=%fused_computation.6 | convolution fusion | flops 1208745984 | bytes 6684672 | tf_op jit(solution)/shard_map/dot_general | solution.py:66
  48.9 2.2 fusion.45
  51.3 53.0 %all-reduce.5.cloned.1.call-done = f32[1024,32]{0,1:T(8,128)} async-done(((f32[1024,32]{0,1:T(8,128)}), f32[1024,32]{0,1:T(8,128)}) %all-reduce.5.cloned.1.call-update) | async-done | bytes 131088 | tf_op jit(solution)/shard_map/psum | solution.py:13
  104.3 6.8 %scatter_custom_fusion = s32[3072]{0:T(1024)} fusion(s32[1536]{0:T(1024)S(1)} %broadcast_select_fusion, s32[1536]{0:T(1024)S(1)} %get-tuple-element.13, s32[]{:T(128)} %constant.83.clone.1), kind=kCustom, calls=%fused_computation.70 | custom fusion | bytes 12292
  111.1 4.6 %all-to-all-start = ((s32[4,1,768]{2,1,0:T(1,128)}), s32[4,1,768]{2,1,0:T(1,128)S(1)}, u32[]{:S(2)}, u32[]{:S(2)}) async-start(s32[4,1,768]{2,1,0:T(1,128)} %bitcast.13), calls=%async_computation | async-start | bytes 24576 | tf_op jit(solution)/shard_map/all_to_all | solution.py:39
  115.7 5.7 %scatter_custom_fusion.1 = bf16[3072,128]{1,0:T(8,128)(2,1)} fusion(s32[1536]{0:T(1024)S(1)} %broadcast_select_fusion, bf16[1536,128]{1,0:T(8,128)(2,1)} %param.19, bf16[]{:T(256)} %constant.89.clone.1), kind=kCustom, calls=%fused_computation.11 | custom fusion | bytes 786944
  121.4 19.2 %all-reduce.7.cloned.1.call-done = f32[1024,32]{0,1:T(8,128)} async-done(((f32[1024,32]{0,1:T(8,128)}), f32[1024,32]{0,1:T(8,128)}) %all-reduce.7.cloned.1.call-update) | async-done | bytes 131088 | tf_op jit(solution)/shard_map/psum | solution.py:14
  140.6 1.2 fusion.15
  141.9 2.9 cholesky.44
  146.0 3.5 %all-to-all-start.1 = ((bf16[4,768,128]{2,1,0:T(8,128)(2,1)}), bf16[4,768,128]{2,1,0:T(8,128)(2,1)S(1)}, u32[]{:S(2)}, u32[]{:S(2)}) async-start(bf16[4,768,128]{2,1,0:T(8,128)(2,1)} %bitcast.15), calls=%async_computation.1 | async-start | bytes 1572864 | tf_op jit(solution)/shard_map/all_to_all | solution.py:38
  149.5 1.3 compare_reduce_fusion.1
  150.8 1.3 fusion.27
  152.1 3.2 custom-call.6
  155.2 1.2 fusion.9
  156.5 1.6 fusion.46
  158.1 21.1 %psum.44 = f32[384,32]{0,1:T(8,128)} all-reduce(f32[384,32]{0,1:T(8,128)} %fusion.46), channel_id=1, replica_groups=mesh['rep'=4,'tp'=8] {'rep'}, use_global_device_ids=true, to_apply=%region_4.0 | all-reduce | flops 12288 | bytes 98304 | tf_op jit(solution)/shard_map/psum | solution.py:83
  179.2 3.0 fusion.21
  182.5 51.0 %all-reduce.9.cloned.1.call-done = f32[1024,32]{0,1:T(8,128)} async-done(((f32[1024,32]{0,1:T(8,128)}), f32[1024,32]{0,1:T(8,128)}) %all-reduce.9.cloned.1.call-update) | async-done | bytes 131088 | tf_op jit(solution)/shard_map/psum | solution.py:13
  233.5 2.5 fusion.3
  236.0 33.6 %all-reduce.11.cloned.1.call-done = f32[1024,32]{0,1:T(8,128)} async-done(((f32[1024,32]{0,1:T(8,128)}), f32[1024,32]{0,1:T(8,128)}) %all-reduce.11.cloned.1.call-update) | async-done | bytes 131088 | tf_op jit(solution)/shard_map/psum | solution.py:14
  269.6 1.2 fusion.12
  270.9 2.9 cholesky.55
  275.2 2.4 custom-call.7
  277.6 1.2 fusion.7
  279.8 18.1 %psum.47 = f32[384,32]{0,1:T(8,128)S(1)} all-reduce(f32[384,32]{0,1:T(8,128)S(1)} %fusion.47), channel_id=1, replica_groups=mesh['rep'=4,'tp'=8] {'rep'}, use_global_device_ids=true, to_apply=%region_7.10 | all-reduce | flops 12288 | bytes 98304 | tf_op jit(solution)/shard_map/psum | solution.py:83
  298.0 1.5 fusion.48
  299.5 1.1 fusion.4
  300.6 1.0 fusion.44
  301.6 17.5 %all_gather.7 = bf16[1024,384]{1,0:T(8,128)(2,1)S(1)} all-gather(bf16[256,384]{1,0:T(8,128)(2,1)S(1)} %get-tuple-element.10), channel_id=1, replica_groups=mesh['rep'=4,'tp'=8] {'rep'}, dimensions={0}, use_global_device_ids=true | all-gather | bytes 983040 | tf_op jit(solution)/shard_map/all_gather | solution.py:92
  (57 shorter events, 7.2 us)
Async XLA Ops:
  7.2 37.8 %copy-start = (bf16[1536,384]{1,0:T(8,128)(2,1)S(1)}, bf16[1536,384]{1,0:T(8,128)(2,1)}, u32[]{:S(2)}) copy-start(bf16[1536,384]{1,0:T(8,128)(2,1)} %param.14) | copy-start | bytes 3538948
  7.2 1.5 copy-start.1
  7.2 37.8 %all-gather.2.cloned.1.call-start = ((), (), s32[]{:S(2)}) async-start(), calls=%async_computation.2 | async-start | bytes 3538944 | tf_op jit(solution)/shard_map/all_gather | solution.py:67
  7.9 96.4 %all-reduce.5.cloned.1.call-start = ((), (), s32[]{:S(2)}) async-start(), calls=%async_computation.3 | async-start | bytes 262144 | tf_op jit(solution)/shard_map/psum | solution.py:13
  8.7 10.2 %copy-start.9 = (s32[2]{0:T(128)S(1)}, s32[2]{0:T(128)}, u32[]{:S(2)}) copy-start(s32[2]{0:T(128)} %constant.95) | copy-start | bytes 28
  19.0 29.9 %copy-start.5 = (f32[384,32]{0,1:T(8,128)S(1)}, f32[384,32]{0,1:T(8,128)}, u32[]{:S(2)}) copy-start(f32[384,32]{0,1:T(8,128)} %param.16) | copy-start | bytes 147460
  48.9 2.3 copy-start.8
  51.2 89.4 %all-reduce.7.cloned.1.call-start = ((), (), s32[]{:S(2)}) async-start(), calls=%async_computation.4 | async-start | bytes 262144 | tf_op jit(solution)/shard_map/psum | solution.py:14
  111.1 34.3 %all-to-all-start = ((s32[4,1,768]{2,1,0:T(1,128)}), s32[4,1,768]{2,1,0:T(1,128)S(1)}, u32[]{:S(2)}, u32[]{:S(2)}) async-start(s32[4,1,768]{2,1,0:T(1,128)} %bitcast.13), calls=%async_computation | async-start | bytes 24576 | tf_op jit(solution)/shard_map/all_to_all | solution.py:39
  145.4 0.6 copy-start.6
  146.0 87.5 %all-to-all-start.1 = ((bf16[4,768,128]{2,1,0:T(8,128)(2,1)}), bf16[4,768,128]{2,1,0:T(8,128)(2,1)S(1)}, u32[]{:S(2)}, u32[]{:S(2)}) async-start(bf16[4,768,128]{2,1,0:T(8,128)(2,1)} %bitcast.15), calls=%async_computation.1 | async-start | bytes 1572864 | tf_op jit(solution)/shard_map/all_to_all | solution.py:38
  149.5 84.0 %all-reduce.9.cloned.1.call-start = ((), (), s32[]{:S(2)}) async-start(), calls=%async_computation.5 | async-start | bytes 262144 | tf_op jit(solution)/shard_map/psum | solution.py:13
  156.5 77.1 %copy-start.7 = (s32[4,1,768]{2,1,0:T(1,128)S(1)}, s32[4,1,768]{2,1,0:T(1,128)}, u32[]{:S(2)}) copy-start(s32[4,1,768]{2,1,0:T(1,128)} %copy-done.6) | copy-start | bytes 36868
  182.3 87.3 %all-reduce.11.cloned.1.call-start = ((), (), s32[]{:S(2)}) async-start(), calls=%async_computation.6 | async-start | bytes 262144 | tf_op jit(solution)/shard_map/psum | solution.py:14
  298.0 2.6 copy-start.4
  299.4 1.2 copy-start.2
  299.5 1.2 copy-start.3
Sparse Core Ops, SparseCore 0:
  9.9 35.0 all-gather.1
  51.3 52.9 all-reduce.4
  106.7 33.8 all-reduce.6
  182.4 51.0 all-reduce.8
  235.8 33.8 all-reduce.10
